TPU v7x, 128 devices: a whole 4x4x4 slice. The times are simulated.
128 devices in a mesh: expo: 8 (over z, core), sky: 16 (over x, y).
Axes of the slice: x: 4, y: 4, z: 4, core: 2. Of those that a mesh axis runs over, the one named last changes fastest.
Arguments:
- samples: bfloat16 [1024, 32, 256], P('sky'), may hold values from -0.75 to 0.75
- basis: bfloat16 [256, 1024], replicated, may hold values from -3 to 3
- operators: bfloat16 [1024, 1024, 1024], P(('expo', 'sky')), may hold values from -0.1875 to 0.1875
- cutouts: float32 [1024, 16, 1024], P(('expo', 'sky')), may hold values from -6 to 6
- pixel_weights: float32 [1024, 16, 1024], P(('expo', 'sky')), may hold values from 0.25 to 4
- detections: int32 [8, 16, 16, 12], P('expo', 'sky'), may hold values from -1 to 63, as said below
- intersections: int32 [1024, 16], P(('expo', 'sky')), may hold values from -1 to 191, as said below
Outputs:
- loglik: float32 [1024, 32], P('sky', 'expo')
- coeff_grads: float32 [1024, 32, 256], P('sky', 'expo')
Inputs may be any that keep to these rules, and one draw needn't show every extreme that they name: In detections[e, s, c], the live slots (values 0 or more) come first; -1 marks the rest. For every device (e, c), the live slots over all s total exactly 96, and one s fills all 12. A galaxy may stand in several slots. `intersections`: on device (e, c), a slot r = s * 12 + j is live exactly when detections[e, s, c, j] >= 0, and each live slot stands at exactly one position of the device's tiles; -1 marks empty positions. One tile of every device has all 16 positions filled.
All inputs are finite; a program needn't handle non-finite values.
Results may differ from a plain program's by a relative error of at most 0.0017.
Values may be sent and summed in bfloat16 or wider, within the bound.
No kernel may reach another device: no remote copies, remote signals or barrier semaphores. Data moves between devices by JAX's collectives and lax.ppermute only.
A program may use at most 128 MiB of HBM per device.

v0:
```python
import jax
import jax.numpy as jnp
from jax import lax
from jax.sharding import PartitionSpec as P

N_CHUNKS = 2
LANE = 128


def select(rows, cols):
    return (rows[:, None] == cols[None, :]).astype(jnp.bfloat16)


def per_device(samples, basis, operators, cutouts, pixel_weights, detections, intersections):
    tiles_here, tile_cap, pixels = cutouts.shape
    coeff_dim = basis.shape[0]
    galaxy_count, sample_count, _unused = samples.shape
    sky_count = lax.axis_size("sky")
    expo_count = lax.axis_size("expo")
    send_cap = detections.shape[3]
    slot_count = sky_count * send_cap
    per_expo = sample_count // expo_count
    chunk_size = per_expo // N_CHUNKS
    chunk_samples = expo_count * chunk_size
    positions = tiles_here * tile_cap
    devices = expo_count * sky_count

    listed_all = lax.all_gather(
        detections.reshape(sky_count, send_cap), "expo", axis=0, tiled=False
    )
    sent_rows = lax.dynamic_index_in_dim(listed_all, lax.axis_index("expo"), 0, keepdims=False)
    listed_flat = listed_all.reshape(-1)
    onehot = (listed_flat[None, :] == jnp.arange(galaxy_count, dtype=jnp.int32)[:, None]).astype(
        jnp.float32
    )
    onehot_k = (
        onehot[:, None, :, None]
        * jnp.eye(chunk_size, dtype=jnp.float32)[None, :, None, :]
    ).reshape(galaxy_count * chunk_size, -1)

    arranged = samples.reshape(galaxy_count, expo_count, N_CHUNKS, chunk_size, coeff_dim)
    arranged = arranged.transpose(2, 1, 3, 0, 4).reshape(N_CHUNKS, chunk_samples, galaxy_count, -1)
    send_select = select(sent_rows.reshape(-1), jnp.arange(galaxy_count, dtype=jnp.int32))
    send_select = jnp.broadcast_to(send_select[None], (chunk_samples,) + send_select.shape)
    pick = jnp.maximum(intersections, 0).reshape(-1)
    pick_select = select(pick, jnp.arange(slot_count, dtype=jnp.int32))
    pick_select = jnp.broadcast_to(pick_select[None], (chunk_samples,) + pick_select.shape)
    live = intersections >= 0
    target = jnp.where(live, intersections, slot_count).reshape(-1)
    holder = jnp.full((slot_count,), positions, jnp.int32)
    holder = holder.at[target].set(jnp.arange(positions, dtype=jnp.int32), mode="drop")
    k_ids = jnp.arange(chunk_size, dtype=jnp.int32)
    back_src = (k_ids[None, :] * positions + holder[:, None]).reshape(-1)
    back_src = jnp.where(jnp.repeat(holder, chunk_size) < positions, back_src, -1)
    back_select = select(back_src, jnp.arange(chunk_size * positions, dtype=jnp.int32))
    back_select = jnp.broadcast_to(
        back_select.astype(jnp.float32)[None], (expo_count,) + back_select.shape
    )

    grad_pieces = []
    like_rows = []
    for chunk in range(N_CHUNKS):
        sent = lax.dot_general(
            send_select,
            arranged[chunk],
            (((2,), (1,)), ((0,), (0,))),
            preferred_element_type=jnp.float32,
        ).astype(jnp.bfloat16)
        sent = sent.transpose(1, 0, 2).reshape(-1, coeff_dim)
        incoming = lax.all_to_all(sent, "sky", split_axis=0, concat_axis=0, tiled=True)
        by_sample = incoming.reshape(slot_count, chunk_samples, coeff_dim).transpose(1, 0, 2)
        picked = lax.dot_general(
            pick_select,
            by_sample,
            (((2,), (1,)), ((0,), (0,))),
            preferred_element_type=jnp.float32,
        ).astype(jnp.bfloat16)
        picked = picked.reshape(chunk_samples, tiles_here, tile_cap, coeff_dim)
        picked = picked.transpose(1, 0, 2, 3).reshape(-1, coeff_dim)
        rendered = jnp.dot(picked, basis, preferred_element_type=jnp.float32).astype(jnp.bfloat16)
        rendered = rendered.reshape(tiles_here, chunk_samples * tile_cap, pixels)
        model = jnp.einsum("tnp,tpq->tnq", rendered, operators, preferred_element_type=jnp.float32)
        model = model.reshape(tiles_here, chunk_samples, tile_cap, pixels)
        resid = model - cutouts[:, None, :, :]
        weighted = pixel_weights[:, None, :, :] * resid
        pair_like = -0.5 / pixels * jnp.sum(weighted * resid, axis=-1)
        scaled = weighted.astype(jnp.bfloat16).reshape(tiles_here, chunk_samples * tile_cap, pixels)
        backed = jnp.einsum(
            "tnq,tpq->tnp", scaled, operators, preferred_element_type=jnp.float32
        ).astype(jnp.bfloat16)
        pair_grad = (
            -1.0
            / pixels
            * lax.dot_general(
                backed.reshape(-1, pixels),
                basis,
                (((1,), (1,)), ((), ())),
                preferred_element_type=jnp.float32,
            )
        )
        grad_src = pair_grad.reshape(tiles_here, expo_count, chunk_size, tile_cap, coeff_dim)
        grad_src = grad_src.transpose(1, 2, 0, 3, 4).reshape(expo_count, -1, coeff_dim)
        send_back = lax.dot_general(
            back_select,
            grad_src,
            (((2,), (1,)), ((0,), (0,))),
            precision=lax.Precision.HIGHEST,
            preferred_element_type=jnp.float32,
        ).reshape(-1, coeff_dim)
        back = lax.all_to_all(send_back, ("expo", "sky"), split_axis=0, concat_axis=0, tiled=True)
        grads = jnp.dot(onehot_k, back, precision=lax.Precision.HIGHEST)
        grad_pieces.append(grads.reshape(galaxy_count, chunk_size, coeff_dim))
        like_rows.append(
            pair_like.reshape(tiles_here, expo_count, chunk_size, tile_cap).transpose(1, 2, 0, 3)
        )
    likes = jnp.stack(like_rows, axis=1).reshape(expo_count, per_expo, positions)
    likes = jnp.take(likes, holder, axis=2, mode="fill", fill_value=0.0).transpose(0, 2, 1)
    like_width = send_cap * per_expo
    likes = likes.reshape(devices, like_width)
    likes = jnp.pad(likes, ((0, 0), (0, -like_width % LANE)))
    back_likes = lax.all_to_all(likes, ("expo", "sky"), split_axis=0, concat_axis=0, tiled=True)
    back_likes = back_likes[:, :like_width].reshape(-1, per_expo)
    like_out = jnp.dot(onehot, back_likes, precision=lax.Precision.HIGHEST)
    grad_out = jnp.concatenate(grad_pieces, axis=1)
    return (like_out, grad_out)


def solution(mesh):
    placed = (
        P("sky", None, None),
        P(),
        P(("expo", "sky"), None, None),
        P(("expo", "sky"), None, None),
        P(("expo", "sky"), None, None),
        P("expo", "sky", None, None),
        P(("expo", "sky"), None),
    )
    return jax.shard_map(
        per_device,
        mesh=mesh,
        in_specs=placed,
        out_specs=(P("sky", "expo"), P("sky", "expo", None)),
        check_vma=False,
    )
```

profile of v0, /device:TPU:1, one launch (start us, length us, event | category | flops | bytes accessed | tf_op | source)
XLA Modules:
  0.0 244.5 jit_solution(12987674287924156080)
XLA Ops:
  0.6 0.0 copy-start
  0.6 15.7 %all-gather = s32[8,1,16,12]{2,1,3,0:T(1,128)S(1)} all-gather(s32[1,1,16,12]{2,1,3,0:T(1,128)} %param.12), channel_id=2, replica_groups=mesh['expo'=8,'sky'=16] {'expo'}, dimensions={0}, use_global_device_ids=true | all-gather | bytes 6912 | tf_op jit(solution)/shard_map/all_gather | solution.py:28
  16.4 0.1 copy.45
  16.5 0.1 eq.89
  16.6 1.5 reshape.291
  18.0 0.6 copy.76
  18.6 0.1 fusion.46
  18.7 0.6 fusion.27
  19.3 2.0 copy.50
  21.4 6.8 %all-to-all-start.1 = ((bf16[16,192,256]{2,1,0:T(8,128)(2,1)}), bf16[16,192,256]{2,1,0:T(8,128)(2,1)S(1)}, u32[]{:S(2)}, u32[]{:S(2)}) async-start(bf16[16,192,256]{2,1,0:T(8,128)(2,1)} %bitcast.17), calls=%async_computation.1 | async-start | bytes 3145728 | tf_op jit(solution)/shard_map/all_to_all | solution.py:70
  28.2 0.0 copy-start.3
  28.2 0.6 fusion.26
  28.8 2.0 copy.47
  30.8 0.1 reshape.290
  30.9 1.0 scatter_custom_fusion
  31.9 19.6 %all-to-all-done.1 = bf16[16,192,256]{2,1,0:T(8,128)(2,1)S(1)} async-done(((bf16[16,192,256]{2,1,0:T(8,128)(2,1)}), bf16[16,192,256]{2,1,0:T(8,128)(2,1)S(1)}, u32[]{:S(2)}, u32[]{:S(2)}) %all-to-all-start.1) | async-done | bytes 1572896 | tf_op jit(solution)/shard_map/all_to_all | solution.py:70
  51.5 4.9 %all-to-all-start = ((bf16[16,192,256]{2,1,0:T(8,128)(2,1)}), bf16[16,192,256]{2,1,0:T(8,128)(2,1)}, u32[]{:S(2)}, u32[]{:S(2)}) async-start(bf16[16,192,256]{2,1,0:T(8,128)(2,1)} %bitcast.5), calls=%async_computation | async-start | bytes 3145728 | tf_op jit(solution)/shard_map/all_to_all | solution.py:70
  56.4 0.1 eq.85
  56.5 0.1 add_select_fusion
  56.7 0.1 select_n.49
  56.8 0.1 fusion.40
  57.0 0.7 fusion.23
  57.6 0.1 copy.52
  57.7 19.5 %all-to-all-done = bf16[16,192,256]{2,1,0:T(8,128)(2,1)} async-done(((bf16[16,192,256]{2,1,0:T(8,128)(2,1)}), bf16[16,192,256]{2,1,0:T(8,128)(2,1)}, u32[]{:S(2)}, u32[]{:S(2)}) %all-to-all-start) | async-done | bytes 1572896 | tf_op jit(solution)/shard_map/all_to_all | solution.py:70
  77.2 2.1 fusion.20
  79.3 0.1 copy.49
  79.4 1.3 convolution_convert_fusion
  80.6 3.2 %convolution_convert_fusion.1 = bf16[2048,1024]{1,0:T(8,128)(2,1)} fusion(bf16[2048,256]{1,0:T(8,128)(2,1)S(1)} %bitcast.130, bf16[256,1024]{1,0:T(8,128)(2,1)S(1)} %copy-done), kind=kOutput, calls=%fused_computation.13 | convolution fusion | flops 1075838976 | bytes 5767168 | tf_op jit(solution)/shard_map/dot_general | solution.py:80
  83.9 12.7 %fusion.47 = f32[8,256,1024]{2,1,0:T(8,128)} fusion(bf16[8,256,1024]{2,1,0:T(8,128)(2,1)S(1)} %bitcast.124, bf16[8,1024,1024]{2,1,0:T(8,128)(2,1)} %param.9), kind=kOutput, calls=%fused_computation.78 | convolution fusion | flops 4294967296 | bytes 29360128 | tf_op jit(solution)/shard_map/tnp,tpq->tnq/dot_general | solution.py:82
  96.5 14.2 %fusion.5 = (f32[8,256]{1,0:T(8,128)S(1)}, f32[8,256]{1,0:T(8,128)S(1)}, bf16[8,256,1024]{2,1,0:T(8,128)(2,1)}, bf16[8,256,1024]{2,1,0:T(8,128)(2,1)}) fusion(f32[8,16,1024]{2,1,0:T(8,128)S(1)} %copy-done.1, f32[8,16,1024]{2,1,0:T(8,128)S(1)} %copy-done.2, f32[8,256,1024]{2,1,0:T(8,128)} %fusion.47, bf16[8,256,1024]{2,1,0:T(8,128)(2,1)} %bitcast.123, ...), kind=kOutput, calls=%fused_computation.11 | convolution fusion | flops 4315934720 | bytes 38813696 | tf_op jit(solution)/shard_map/tnp,tpq->tnq/dot_general | solution.py:82
  110.8 0.1 mul.88
  110.9 0.1 mul.92
  111.0 0.1 pad_maximum_fusion.1
  111.1 0.2 copy.61
  111.3 0.9 gather_fusion
  112.2 0.3 select_bitcast_fusion
  112.5 1.2 copy.55
  113.7 0.3 reshape.301
  114.0 0.6 pad.4
  114.6 9.0 %all-to-all-start.2 = ((f32[128,1,128]{2,1,0:T(1,128)}), f32[128,1,128]{2,1,0:T(1,128)S(1)}, u32[]{:S(2)}, u32[]{:S(2)}) async-start(f32[128,1,128]{2,1,0:T(1,128)} %bitcast.29), calls=%async_computation.2 | async-start | bytes 131072 | tf_op jit(solution)/shard_map/all_to_all | solution.py:121
  123.6 10.9 %convolution_convert_fusion.2 = bf16[8,256,1024]{2,1,0:T(8,128)(2,1)} fusion(bf16[8,256,1024]{2,1,0:T(8,128)(2,1)} %get-tuple-element.13, bf16[8,1024,1024]{2,1,0:T(8,128)(2,1)} %param.9), kind=kOutput, calls=%fused_computation.16 | convolution fusion | flops 4297064448 | bytes 25165824 | tf_op jit(solution)/shard_map/tnq,tpq->tnp/dot_general | solution.py:88
  134.5 3.5 %convolution_multiply_fusion = f32[2048,256]{1,0:T(8,128)S(1)} fusion(bf16[2048,1024]{1,0:T(8,128)(2,1)} %bitcast.144, bf16[256,1024]{1,0:T(8,128)(2,1)S(1)} %copy-done), kind=kOutput, calls=%fused_computation.14 | convolution fusion | flops 1074266112 | bytes 6815744 | tf_op jit(solution)/shard_map/dot_general | solution.py:94
  138.0 0.2 copy.59
  138.2 4.3 %fusion.16 = f32[8,384,256]{2,1,0:T(8,128)} fusion(f32[8,256,256]{2,1,0:T(8,128)S(1)} %bitcast.128, f32[384,256]{1,0:T(8,128)S(1)} %fusion.40), kind=kOutput, calls=%fused_computation.30 | convolution fusion | flops 2415919104 | bytes 5636096 | tf_op jit(solution)/shard_map/dot_general | solution.py:103
  142.5 10.5 %all-to-all-start.4 = ((f32[128,24,256]{2,1,0:T(8,128)}), f32[128,24,256]{2,1,0:T(8,128)}, u32[]{:S(2)}, u32[]{:S(2)}) async-start(f32[128,24,256]{2,1,0:T(8,128)} %bitcast.126), calls=%async_computation.4 | async-start | bytes 6291456 | tf_op jit(solution)/shard_map/all_to_all | solution.py:110
  153.1 10.9 %convolution_convert_fusion.3 = bf16[8,256,1024]{2,1,0:T(8,128)(2,1)} fusion(bf16[8,256,1024]{2,1,0:T(8,128)(2,1)} %get-tuple-element.12, bf16[8,1024,1024]{2,1,0:T(8,128)(2,1)} %param.9), kind=kOutput, calls=%fused_computation.17 | convolution fusion | flops 4297064448 | bytes 25165824 | tf_op jit(solution)/shard_map/tnq,tpq->tnp/dot_general | solution.py:88
  163.9 3.5 %convolution_multiply_fusion.1 = f32[2048,256]{1,0:T(8,128)S(1)} fusion(bf16[2048,1024]{1,0:T(8,128)(2,1)} %bitcast.145, bf16[256,1024]{1,0:T(8,128)(2,1)S(1)} %copy-done), kind=kOutput, calls=%fused_computation.15 | convolution fusion | flops 1074266112 | bytes 6815744 | tf_op jit(solution)/shard_map/dot_general | solution.py:94
  167.4 0.2 copy.58
  167.6 4.3 %fusion.18 = f32[8,384,256]{2,1,0:T(8,128)} fusion(f32[8,256,256]{2,1,0:T(8,128)S(1)} %bitcast.127, f32[384,256]{1,0:T(8,128)S(1)} %fusion.40), kind=kOutput, calls=%fused_computation.32 | convolution fusion | flops 2415919104 | bytes 5636096 | tf_op jit(solution)/shard_map/dot_general | solution.py:103
  171.9 21.6 %all-to-all-done.4 = f32[128,24,256]{2,1,0:T(8,128)} async-done(((f32[128,24,256]{2,1,0:T(8,128)}), f32[128,24,256]{2,1,0:T(8,128)}, u32[]{:S(2)}, u32[]{:S(2)}) %all-to-all-start.4) | async-done | bytes 3145760 | tf_op jit(solution)/shard_map/all_to_all | solution.py:110
  193.5 5.6 %all-to-all-start.3 = ((f32[128,24,256]{2,1,0:T(8,128)}), f32[128,24,256]{2,1,0:T(8,128)}, u32[]{:S(2)}, u32[]{:S(2)}) async-start(f32[128,24,256]{2,1,0:T(8,128)} %bitcast.125), calls=%async_computation.3 | async-start | bytes 6291456 | tf_op jit(solution)/shard_map/all_to_all | solution.py:110
  199.1 0.1 copy.44
  199.2 0.1 eq.81
  199.3 0.3 fusion.32
  199.6 0.6 mul.93
  200.2 0.4 copy.57
  200.7 0.1 mul.96
  200.8 0.9 mul.97
  201.7 0.3 reshape.302
  201.9 1.6 fusion.33
  203.5 3.6 %fusion.6 = f32[64,2,256]{2,0,1:T(8,128)S(1)} fusion(f32[3072,256,1]{1,0,2:T(8,128)} %bitcast.45, f32[2,3072]{1,0:T(2,128)S(1)} %mul.97, f32[64,3072]{1,0:T(8,128)S(1)} %copy.57), kind=kOutput, calls=%fused_computation.18 | convolution fusion | flops 1208352768 | bytes 4087808 | tf_op jit(solution)/shard_map/dot_general | solution.py:111
  207.1 32.7 %all-to-all-done.3 = f32[128,24,256]{2,1,0:T(8,128)} async-done(((f32[128,24,256]{2,1,0:T(8,128)}), f32[128,24,256]{2,1,0:T(8,128)}, u32[]{:S(2)}, u32[]{:S(2)}) %all-to-all-start.3) | async-done | bytes 3145760 | tf_op jit(solution)/shard_map/all_to_all | solution.py:110
  239.7 3.6 %fusion.8 = f32[64,2,256]{2,0,1:T(8,128)S(1)} fusion(f32[3072,256,1]{1,0,2:T(8,128)} %bitcast.38, f32[2,3072]{1,0:T(2,128)S(1)} %mul.97, f32[64,3072]{1,0:T(8,128)S(1)} %copy.57), kind=kOutput, calls=%fused_computation.20 | convolution fusion | flops 1208352768 | bytes 4087808 | tf_op jit(solution)/shard_map/dot_general | solution.py:111
  243.3 0.9 copy.60
  (20 shorter events, 0.1 us)
Async XLA Ops:
  0.6 78.7 %copy-start = (bf16[256,1024]{1,0:T(8,128)(2,1)S(1)}, bf16[256,1024]{1,0:T(8,128)(2,1)}, u32[]{:S(2)}) copy-start(bf16[256,1024]{1,0:T(8,128)(2,1)} %param.8) | copy-start | bytes 1572868
  21.4 30.1 %all-to-all-start.1 = ((bf16[16,192,256]{2,1,0:T(8,128)(2,1)}), bf16[16,192,256]{2,1,0:T(8,128)(2,1)S(1)}, u32[]{:S(2)}, u32[]{:S(2)}) async-start(bf16[16,192,256]{2,1,0:T(8,128)(2,1)} %bitcast.17), calls=%async_computation.1 | async-start | bytes 3145728 | tf_op jit(solution)/shard_map/all_to_all | solution.py:70
  28.2 2.7 %copy-start.3 = (s32[8,16]{1,0:T(8,128)S(1)}, s32[8,16]{1,0:T(8,128)}, u32[]{:S(2)}) copy-start(s32[8,16]{1,0:T(8,128)} %param.13) | copy-start | bytes 1540
  51.5 25.7 %all-to-all-start = ((bf16[16,192,256]{2,1,0:T(8,128)(2,1)}), bf16[16,192,256]{2,1,0:T(8,128)(2,1)}, u32[]{:S(2)}, u32[]{:S(2)}) async-start(bf16[16,192,256]{2,1,0:T(8,128)(2,1)} %bitcast.5), calls=%async_computation | async-start | bytes 3145728 | tf_op jit(solution)/shard_map/all_to_all | solution.py:70
  83.9 12.7 %copy-start.1 = (f32[8,16,1024]{2,1,0:T(8,128)S(1)}, f32[8,16,1024]{2,1,0:T(8,128)}, u32[]{:S(2)}) copy-start(f32[8,16,1024]{2,1,0:T(8,128)} %param.10) | copy-start | bytes 1572868
  83.9 12.7 %copy-start.2 = (f32[8,16,1024]{2,1,0:T(8,128)S(1)}, f32[8,16,1024]{2,1,0:T(8,128)}, u32[]{:S(2)}) copy-start(f32[8,16,1024]{2,1,0:T(8,128)} %param.11) | copy-start | bytes 1572868
  114.6 27.9 %all-to-all-start.2 = ((f32[128,1,128]{2,1,0:T(1,128)}), f32[128,1,128]{2,1,0:T(1,128)S(1)}, u32[]{:S(2)}, u32[]{:S(2)}) async-start(f32[128,1,128]{2,1,0:T(1,128)} %bitcast.29), calls=%async_computation.2 | async-start | bytes 131072 | tf_op jit(solution)/shard_map/all_to_all | solution.py:121
  142.5 51.0 %all-to-all-start.4 = ((f32[128,24,256]{2,1,0:T(8,128)}), f32[128,24,256]{2,1,0:T(8,128)}, u32[]{:S(2)}, u32[]{:S(2)}) async-start(f32[128,24,256]{2,1,0:T(8,128)} %bitcast.126), calls=%async_computation.4 | async-start | bytes 6291456 | tf_op jit(solution)/shard_map/all_to_all | solution.py:110
  193.5 46.2 %all-to-all-start.3 = ((f32[128,24,256]{2,1,0:T(8,128)}), f32[128,24,256]{2,1,0:T(8,128)}, u32[]{:S(2)}, u32[]{:S(2)}) async-start(f32[128,24,256]{2,1,0:T(8,128)} %bitcast.125), calls=%async_computation.3 | async-start | bytes 6291456 | tf_op jit(solution)/shard_map/all_to_all | solution.py:110
where the time goes:
time: 249 us; the launch traced here: 244 us
  waiting for transfers between devices  93.3 us (37%)
  matrix products  81.3 us (33%)
  starting transfers between devices  36.8 us (15%)
  blocking collectives  15.7 us (6%)
  local copies, waits for them, and re-layouts  15.1 us (6%)
    all_to_all x2, waiting for transfers between devices, per_device(): lax.all_to_all(send_back, ('expo', 'sky'), split_axis=0, concat_axis=0, t...  54.3 us
    all_to_all x2, waiting for transfers between devices, per_device(): lax.all_to_all(sent, 'sky', split_axis=0, concat_axis=0, tiled=True)  39 us
    dot_general x2, matrix products, per_device(): jnp.einsum('tnp,tpq->tnq', rendered, operators, preferred_element_type=jn...  26.9 us
    dot_general x2, matrix products, per_device(): jnp.einsum('tnq,tpq->tnp', scaled, operators, preferred_element_type=jnp....  21.7 us
    all_to_all x2, starting transfers between devices, per_device(): lax.all_to_all(send_back, ('expo', 'sky'), split_axis=0, concat_axis=0, t...  16.1 us
    all_gather x1, blocking collectives, per_device(): lax.all_gather(detections.reshape(sky_count, send_cap), 'expo', axis=0, t...  15.7 us
    all_to_all x2, starting transfers between devices, per_device(): lax.all_to_all(sent, 'sky', split_axis=0, concat_axis=0, tiled=True)  11.7 us
    all_to_all x1, starting transfers between devices, per_device(): lax.all_to_all(likes, ('expo', 'sky'), split_axis=0, concat_axis=0, tiled...  9.02 us
  transfers between devices with their start and end apart: 5, of which 4 were waited for; matrix products, arithmetic and copies ran while one was open for 21% of the time, Pallas kernels for 0%

commit v1 on v0

--- a/solution.py
+++ b/solution.py
@@ -104,11 +104,11 @@
             back_select,
             grad_src,
             (((2,), (1,)), ((0,), (0,))),
-            precision=lax.Precision.HIGHEST,
+            precision=lax.Precision.HIGH,
             preferred_element_type=jnp.float32,
         ).reshape(-1, coeff_dim)
         back = lax.all_to_all(send_back, ("expo", "sky"), split_axis=0, concat_axis=0, tiled=True)
-        grads = jnp.dot(onehot_k, back, precision=lax.Precision.HIGHEST)
+        grads = jnp.dot(onehot_k, back, precision=lax.Precision.HIGH)
         grad_pieces.append(grads.reshape(galaxy_count, chunk_size, coeff_dim))
         like_rows.append(
             pair_like.reshape(tiles_here, expo_count, chunk_size, tile_cap).transpose(1, 2, 0, 3)

time: 249 us -> 242 us (0.972); the launches traced: 244 us -> 241 us
  matrix products: 81.3 us -> 77.6 us
  transfers between devices with their start and end apart: 5 -> 5, of which waited for: 4 -> 4; matrix products, arithmetic and copies ran while one was open for 21% -> 20% of each run, Pallas kernels for 0% -> 0%
where the time goes in v1:
time: 242 us; the launch traced here: 241 us
  waiting for transfers between devices  95.3 us (39%)
  matrix products  77.6 us (32%)
  starting transfers between devices  35.4 us (15%)
  blocking collectives  15.7 us (6%)
  local copies, waits for them, and re-layouts  15.1 us (6%)
    all_to_all x2, waiting for transfers between devices, per_device(): lax.all_to_all(send_back, ('expo', 'sky'), split_axis=0, concat_axis=0, t...  56.5 us
    all_to_all x2, waiting for transfers between devices, per_device(): lax.all_to_all(sent, 'sky', split_axis=0, concat_axis=0, tiled=True)  38.8 us
    dot_general x2, matrix products, per_device(): jnp.einsum('tnp,tpq->tnq', rendered, operators, preferred_element_type=jn...  26.9 us
    dot_general x2, matrix products, per_device(): jnp.einsum('tnq,tpq->tnp', scaled, operators, preferred_element_type=jnp....  21.7 us
    all_gather x1, blocking collectives, per_device(): lax.all_gather(detections.reshape(sky_count, send_cap), 'expo', axis=0, t...  15.7 us
    all_to_all x2, starting transfers between devices, per_device(): lax.all_to_all(send_back, ('expo', 'sky'), split_axis=0, concat_axis=0, t...  15.3 us
    all_to_all x2, starting transfers between devices, per_device(): lax.all_to_all(sent, 'sky', split_axis=0, concat_axis=0, tiled=True)  11.3 us
    all_to_all x1, starting transfers between devices, per_device(): lax.all_to_all(likes, ('expo', 'sky'), split_axis=0, concat_axis=0, tiled...  8.79 us
  transfers between devices with their start and end apart: 5, of which 4 were waited for; matrix products, arithmetic and copies ran while one was open for 20% of the time, Pallas kernels for 0%

profile of v1, /device:TPU:1, one launch (start us, length us, event | category | flops | bytes accessed | tf_op | source)
XLA Modules:
  0.0 241.1 jit_solution(8387519896690419908)
XLA Ops:
  0.6 0.0 copy-start
  0.6 15.7 %all-gather = s32[8,1,16,12]{2,1,3,0:T(1,128)S(1)} all-gather(s32[1,1,16,12]{2,1,3,0:T(1,128)} %param.12), channel_id=2, replica_groups=mesh['expo'=8,'sky'=16] {'expo'}, dimensions={0}, use_global_device_ids=true | all-gather | bytes 6912 | tf_op jit(solution)/shard_map/all_gather | solution.py:28
  16.4 0.1 copy.45
  16.5 0.1 eq.89
  16.6 1.5 reshape.291
  18.0 0.6 copy.76
  18.6 0.1 fusion.46
  18.7 0.6 fusion.27
  19.4 2.0 copy.50
  21.4 6.8 %all-to-all-start.1 = ((bf16[16,192,256]{2,1,0:T(8,128)(2,1)}), bf16[16,192,256]{2,1,0:T(8,128)(2,1)S(1)}, u32[]{:S(2)}, u32[]{:S(2)}) async-start(bf16[16,192,256]{2,1,0:T(8,128)(2,1)} %bitcast.17), calls=%async_computation.1 | async-start | bytes 3145728 | tf_op jit(solution)/shard_map/all_to_all | solution.py:70
  28.2 0.0 copy-start.3
  28.2 0.6 fusion.26
  28.8 2.0 copy.47
  30.8 0.1 reshape.290
  30.9 1.0 scatter_custom_fusion
  31.9 19.5 %all-to-all-done.1 = bf16[16,192,256]{2,1,0:T(8,128)(2,1)S(1)} async-done(((bf16[16,192,256]{2,1,0:T(8,128)(2,1)}), bf16[16,192,256]{2,1,0:T(8,128)(2,1)S(1)}, u32[]{:S(2)}, u32[]{:S(2)}) %all-to-all-start.1) | async-done | bytes 1572896 | tf_op jit(solution)/shard_map/all_to_all | solution.py:70
  51.4 4.6 %all-to-all-start = ((bf16[16,192,256]{2,1,0:T(8,128)(2,1)}), bf16[16,192,256]{2,1,0:T(8,128)(2,1)}, u32[]{:S(2)}, u32[]{:S(2)}) async-start(bf16[16,192,256]{2,1,0:T(8,128)(2,1)} %bitcast.5), calls=%async_computation | async-start | bytes 3145728 | tf_op jit(solution)/shard_map/all_to_all | solution.py:70
  56.0 0.1 eq.85
  56.1 0.1 add_select_fusion
  56.3 0.1 select_n.49
  56.4 0.1 fusion.40
  56.6 0.7 fusion.23
  57.2 0.1 copy.52
  57.3 19.3 %all-to-all-done = bf16[16,192,256]{2,1,0:T(8,128)(2,1)} async-done(((bf16[16,192,256]{2,1,0:T(8,128)(2,1)}), bf16[16,192,256]{2,1,0:T(8,128)(2,1)}, u32[]{:S(2)}, u32[]{:S(2)}) %all-to-all-start) | async-done | bytes 1572896 | tf_op jit(solution)/shard_map/all_to_all | solution.py:70
  76.6 2.1 fusion.20
  78.7 0.1 copy.49
  78.8 1.3 convolution_convert_fusion
  80.1 3.2 %convolution_convert_fusion.1 = bf16[2048,1024]{1,0:T(8,128)(2,1)} fusion(bf16[2048,256]{1,0:T(8,128)(2,1)S(1)} %bitcast.130, bf16[256,1024]{1,0:T(8,128)(2,1)S(1)} %copy-done), kind=kOutput, calls=%fused_computation.13 | convolution fusion | flops 1075838976 | bytes 5767168 | tf_op jit(solution)/shard_map/dot_general | solution.py:80
  83.3 12.7 %fusion.47 = f32[8,256,1024]{2,1,0:T(8,128)} fusion(bf16[8,256,1024]{2,1,0:T(8,128)(2,1)S(1)} %bitcast.124, bf16[8,1024,1024]{2,1,0:T(8,128)(2,1)} %param.9), kind=kOutput, calls=%fused_computation.78 | convolution fusion | flops 4294967296 | bytes 29360128 | tf_op jit(solution)/shard_map/tnp,tpq->tnq/dot_general | solution.py:82
  96.0 14.2 %fusion.5 = (f32[8,256]{1,0:T(8,128)S(1)}, f32[8,256]{1,0:T(8,128)S(1)}, bf16[8,256,1024]{2,1,0:T(8,128)(2,1)}, bf16[8,256,1024]{2,1,0:T(8,128)(2,1)}) fusion(f32[8,16,1024]{2,1,0:T(8,128)S(1)} %copy-done.1, f32[8,16,1024]{2,1,0:T(8,128)S(1)} %copy-done.2, f32[8,256,1024]{2,1,0:T(8,128)} %fusion.47, bf16[8,256,1024]{2,1,0:T(8,128)(2,1)} %bitcast.123, ...), kind=kOutput, calls=%fused_computation.11 | convolution fusion | flops 4315934720 | bytes 38813696 | tf_op jit(solution)/shard_map/tnp,tpq->tnq/dot_general | solution.py:82
  110.2 0.1 mul.88
  110.3 0.1 mul.92
  110.5 0.1 pad_maximum_fusion.1
  110.6 0.2 copy.61
  110.8 0.9 gather_fusion
  111.6 0.3 select_bitcast_fusion
  111.9 1.2 copy.55
  113.1 0.3 reshape.301
  113.4 0.6 pad.4
  114.0 8.8 %all-to-all-start.2 = ((f32[128,1,128]{2,1,0:T(1,128)}), f32[128,1,128]{2,1,0:T(1,128)S(1)}, u32[]{:S(2)}, u32[]{:S(2)}) async-start(f32[128,1,128]{2,1,0:T(1,128)} %bitcast.29), calls=%async_computation.2 | async-start | bytes 131072 | tf_op jit(solution)/shard_map/all_to_all | solution.py:121
  122.8 10.9 %convolution_convert_fusion.2 = bf16[8,256,1024]{2,1,0:T(8,128)(2,1)} fusion(bf16[8,256,1024]{2,1,0:T(8,128)(2,1)} %get-tuple-element.13, bf16[8,1024,1024]{2,1,0:T(8,128)(2,1)} %param.9), kind=kOutput, calls=%fused_computation.16 | convolution fusion | flops 4297064448 | bytes 25165824 | tf_op jit(solution)/shard_map/tnq,tpq->tnp/dot_general | solution.py:88
  133.7 3.5 %convolution_multiply_fusion = f32[2048,256]{1,0:T(8,128)S(1)} fusion(bf16[2048,1024]{1,0:T(8,128)(2,1)} %bitcast.144, bf16[256,1024]{1,0:T(8,128)(2,1)S(1)} %copy-done), kind=kOutput, calls=%fused_computation.14 | convolution fusion | flops 1074266112 | bytes 6815744 | tf_op jit(solution)/shard_map/dot_general | solution.py:94
  137.2 0.2 copy.59
  137.4 3.2 %fusion.16 = f32[8,384,256]{2,1,0:T(8,128)} fusion(f32[8,256,256]{2,1,0:T(8,128)S(1)} %bitcast.128, f32[384,256]{1,0:T(8,128)S(1)} %fusion.40), kind=kOutput, calls=%fused_computation.30 | convolution fusion | flops 1207959552 | bytes 5636096 | tf_op jit(solution)/shard_map/dot_general | solution.py:103
  140.6 10.2 %all-to-all-start.4 = ((f32[128,24,256]{2,1,0:T(8,128)}), f32[128,24,256]{2,1,0:T(8,128)}, u32[]{:S(2)}, u32[]{:S(2)}) async-start(f32[128,24,256]{2,1,0:T(8,128)} %bitcast.126), calls=%async_computation.4 | async-start | bytes 6291456 | tf_op jit(solution)/shard_map/all_to_all | solution.py:110
  150.7 10.8 %convolution_convert_fusion.3 = bf16[8,256,1024]{2,1,0:T(8,128)(2,1)} fusion(bf16[8,256,1024]{2,1,0:T(8,128)(2,1)} %get-tuple-element.12, bf16[8,1024,1024]{2,1,0:T(8,128)(2,1)} %param.9), kind=kOutput, calls=%fused_computation.17 | convolution fusion | flops 4297064448 | bytes 25165824 | tf_op jit(solution)/shard_map/tnq,tpq->tnp/dot_general | solution.py:88
  161.6 3.5 %convolution_multiply_fusion.1 = f32[2048,256]{1,0:T(8,128)S(1)} fusion(bf16[2048,1024]{1,0:T(8,128)(2,1)} %bitcast.145, bf16[256,1024]{1,0:T(8,128)(2,1)S(1)} %copy-done), kind=kOutput, calls=%fused_computation.15 | convolution fusion | flops 1074266112 | bytes 6815744 | tf_op jit(solution)/shard_map/dot_general | solution.py:94
  165.1 0.2 copy.58
  165.3 3.2 %fusion.18 = f32[8,384,256]{2,1,0:T(8,128)} fusion(f32[8,256,256]{2,1,0:T(8,128)S(1)} %bitcast.127, f32[384,256]{1,0:T(8,128)S(1)} %fusion.40), kind=kOutput, calls=%fused_computation.32 | convolution fusion | flops 1207959552 | bytes 5636096 | tf_op jit(solution)/shard_map/dot_general | solution.py:103
  168.5 23.0 %all-to-all-done.4 = f32[128,24,256]{2,1,0:T(8,128)} async-done(((f32[128,24,256]{2,1,0:T(8,128)}), f32[128,24,256]{2,1,0:T(8,128)}, u32[]{:S(2)}, u32[]{:S(2)}) %all-to-all-start.4) | async-done | bytes 3145760 | tf_op jit(solution)/shard_map/all_to_all | solution.py:110
  191.4 5.1 %all-to-all-start.3 = ((f32[128,24,256]{2,1,0:T(8,128)}), f32[128,24,256]{2,1,0:T(8,128)}, u32[]{:S(2)}, u32[]{:S(2)}) async-start(f32[128,24,256]{2,1,0:T(8,128)} %bitcast.125), calls=%async_computation.3 | async-start | bytes 6291456 | tf_op jit(solution)/shard_map/all_to_all | solution.py:110
  196.5 0.1 copy.44
  196.7 0.1 eq.81
  196.8 0.3 fusion.32
  197.0 0.6 mul.93
  197.6 0.4 copy.57
  198.1 0.1 mul.96
  198.2 0.9 mul.97
  199.1 0.3 reshape.302
  199.4 1.6 fusion.33
  200.9 2.8 %fusion.6 = f32[64,2,256]{2,0,1:T(8,128)S(1)} fusion(f32[3072,256,1]{1,0,2:T(8,128)} %bitcast.45, f32[2,3072]{1,0:T(2,128)S(1)} %mul.97, f32[64,3072]{1,0:T(8,128)S(1)} %copy.57), kind=kOutput, calls=%fused_computation.18 | convolution fusion | flops 604372992 | bytes 4087808 | tf_op jit(solution)/shard_map/dot_general | solution.py:111
  203.8 33.6 %all-to-all-done.3 = f32[128,24,256]{2,1,0:T(8,128)} async-done(((f32[128,24,256]{2,1,0:T(8,128)}), f32[128,24,256]{2,1,0:T(8,128)}, u32[]{:S(2)}, u32[]{:S(2)}) %all-to-all-start.3) | async-done | bytes 3145760 | tf_op jit(solution)/shard_map/all_to_all | solution.py:110
  237.3 2.8 %fusion.8 = f32[64,2,256]{2,0,1:T(8,128)S(1)} fusion(f32[3072,256,1]{1,0,2:T(8,128)} %bitcast.38, f32[2,3072]{1,0:T(2,128)S(1)} %mul.97, f32[64,3072]{1,0:T(8,128)S(1)} %copy.57), kind=kOutput, calls=%fused_computation.20 | convolution fusion | flops 604372992 | bytes 4087808 | tf_op jit(solution)/shard_map/dot_general | solution.py:111
  240.2 0.9 copy.60
  (20 shorter events, 0.1 us)
Async XLA Ops:
  0.6 78.2 %copy-start = (bf16[256,1024]{1,0:T(8,128)(2,1)S(1)}, bf16[256,1024]{1,0:T(8,128)(2,1)}, u32[]{:S(2)}) copy-start(bf16[256,1024]{1,0:T(8,128)(2,1)} %param.8) | copy-start | bytes 1572868
  21.4 30.0 %all-to-all-start.1 = ((bf16[16,192,256]{2,1,0:T(8,128)(2,1)}), bf16[16,192,256]{2,1,0:T(8,128)(2,1)S(1)}, u32[]{:S(2)}, u32[]{:S(2)}) async-start(bf16[16,192,256]{2,1,0:T(8,128)(2,1)} %bitcast.17), calls=%async_computation.1 | async-start | bytes 3145728 | tf_op jit(solution)/shard_map/all_to_all | solution.py:70
  28.2 2.7 %copy-start.3 = (s32[8,16]{1,0:T(8,128)S(1)}, s32[8,16]{1,0:T(8,128)}, u32[]{:S(2)}) copy-start(s32[8,16]{1,0:T(8,128)} %param.13) | copy-start | bytes 1540
  51.4 25.2 %all-to-all-start = ((bf16[16,192,256]{2,1,0:T(8,128)(2,1)}), bf16[16,192,256]{2,1,0:T(8,128)(2,1)}, u32[]{:S(2)}, u32[]{:S(2)}) async-start(bf16[16,192,256]{2,1,0:T(8,128)(2,1)} %bitcast.5), calls=%async_computation | async-start | bytes 3145728 | tf_op jit(solution)/shard_map/all_to_all | solution.py:70
  83.3 12.7 %copy-start.1 = (f32[8,16,1024]{2,1,0:T(8,128)S(1)}, f32[8,16,1024]{2,1,0:T(8,128)}, u32[]{:S(2)}) copy-start(f32[8,16,1024]{2,1,0:T(8,128)} %param.10) | copy-start | bytes 1572868
  83.3 12.7 %copy-start.2 = (f32[8,16,1024]{2,1,0:T(8,128)S(1)}, f32[8,16,1024]{2,1,0:T(8,128)}, u32[]{:S(2)}) copy-start(f32[8,16,1024]{2,1,0:T(8,128)} %param.11) | copy-start | bytes 1572868
  114.0 26.5 %all-to-all-start.2 = ((f32[128,1,128]{2,1,0:T(1,128)}), f32[128,1,128]{2,1,0:T(1,128)S(1)}, u32[]{:S(2)}, u32[]{:S(2)}) async-start(f32[128,1,128]{2,1,0:T(1,128)} %bitcast.29), calls=%async_computation.2 | async-start | bytes 131072 | tf_op jit(solution)/shard_map/all_to_all | solution.py:121
  140.6 50.8 %all-to-all-start.4 = ((f32[128,24,256]{2,1,0:T(8,128)}), f32[128,24,256]{2,1,0:T(8,128)}, u32[]{:S(2)}, u32[]{:S(2)}) async-start(f32[128,24,256]{2,1,0:T(8,128)} %bitcast.126), calls=%async_computation.4 | async-start | bytes 6291456 | tf_op jit(solution)/shard_map/all_to_all | solution.py:110
  191.4 45.9 %all-to-all-start.3 = ((f32[128,24,256]{2,1,0:T(8,128)}), f32[128,24,256]{2,1,0:T(8,128)}, u32[]{:S(2)}, u32[]{:S(2)}) async-start(f32[128,24,256]{2,1,0:T(8,128)} %bitcast.125), calls=%async_computation.3 | async-start | bytes 6291456 | tf_op jit(solution)/shard_map/all_to_all | solution.py:110

commit v2 on v1

--- a/solution.py
+++ b/solution.py
@@ -120,7 +120,7 @@
     likes = jnp.pad(likes, ((0, 0), (0, -like_width % LANE)))
     back_likes = lax.all_to_all(likes, ("expo", "sky"), split_axis=0, concat_axis=0, tiled=True)
     back_likes = back_likes[:, :like_width].reshape(-1, per_expo)
-    like_out = jnp.dot(onehot, back_likes, precision=lax.Precision.HIGHEST)
+    like_out = jnp.dot(onehot, back_likes, precision=lax.Precision.HIGH)
     grad_out = jnp.concatenate(grad_pieces, axis=1)
     return (like_out, grad_out)
 

time: 242 us -> 242 us (level)
  no operation moved by 1% of the time
where the time goes in v2:
time: 242 us; the launch traced here: 241 us
  waiting for transfers between devices  95.5 us (39%)
  matrix products  77.4 us (32%)
  starting transfers between devices  35.4 us (15%)
  blocking collectives  15.7 us (6%)
  local copies, waits for them, and re-layouts  15.1 us (6%)
    all_to_all x2, waiting for transfers between devices, per_device(): lax.all_to_all(send_back, ('expo', 'sky'), split_axis=0, concat_axis=0, t...  56.7 us
    all_to_all x2, waiting for transfers between devices, per_device(): lax.all_to_all(sent, 'sky', split_axis=0, concat_axis=0, tiled=True)  38.8 us
    dot_general x2, matrix products, per_device(): jnp.einsum('tnp,tpq->tnq', rendered, operators, preferred_element_type=jn...  26.9 us
    dot_general x2, matrix products, per_device(): jnp.einsum('tnq,tpq->tnp', scaled, operators, preferred_element_type=jnp....  21.7 us
    all_gather x1, blocking collectives, per_device(): lax.all_gather(detections.reshape(sky_count, send_cap), 'expo', axis=0, t...  15.7 us
    all_to_all x2, starting transfers between devices, per_device(): lax.all_to_all(send_back, ('expo', 'sky'), split_axis=0, concat_axis=0, t...  15.3 us
    all_to_all x2, starting transfers between devices, per_device(): lax.all_to_all(sent, 'sky', split_axis=0, concat_axis=0, tiled=True)  11.3 us
    all_to_all x1, starting transfers between devices, per_device(): lax.all_to_all(likes, ('expo', 'sky'), split_axis=0, concat_axis=0, tiled...  8.79 us
  transfers between devices with their start and end apart: 5, of which 4 were waited for; matrix products, arithmetic and copies ran while one was open for 20% of the time, Pallas kernels for 0%

profile of v2, /device:TPU:1, one launch (start us, length us, event | category | flops | bytes accessed | tf_op | source)
XLA Modules:
  0.0 241.1 jit_solution(12805947162352810101)
XLA Ops:
  0.6 0.0 copy-start
  0.6 15.7 %all-gather = s32[8,1,16,12]{2,1,3,0:T(1,128)S(1)} all-gather(s32[1,1,16,12]{2,1,3,0:T(1,128)} %param.12), channel_id=2, replica_groups=mesh['expo'=8,'sky'=16] {'expo'}, dimensions={0}, use_global_device_ids=true | all-gather | bytes 6912 | tf_op jit(solution)/shard_map/all_gather | solution.py:28
  16.4 0.1 copy.45
  16.5 0.1 eq.89
  16.6 1.5 reshape.291
  18.0 0.6 copy.76
  18.6 0.1 fusion.46
  18.7 0.6 fusion.27
  19.4 2.0 copy.50
  21.4 6.8 %all-to-all-start.1 = ((bf16[16,192,256]{2,1,0:T(8,128)(2,1)}), bf16[16,192,256]{2,1,0:T(8,128)(2,1)S(1)}, u32[]{:S(2)}, u32[]{:S(2)}) async-start(bf16[16,192,256]{2,1,0:T(8,128)(2,1)} %bitcast.17), calls=%async_computation.1 | async-start | bytes 3145728 | tf_op jit(solution)/shard_map/all_to_all | solution.py:70
  28.2 0.0 copy-start.3
  28.2 0.6 fusion.26
  28.8 2.0 copy.47
  30.8 0.1 reshape.290
  30.9 1.0 scatter_custom_fusion
  31.9 19.5 %all-to-all-done.1 = bf16[16,192,256]{2,1,0:T(8,128)(2,1)S(1)} async-done(((bf16[16,192,256]{2,1,0:T(8,128)(2,1)}), bf16[16,192,256]{2,1,0:T(8,128)(2,1)S(1)}, u32[]{:S(2)}, u32[]{:S(2)}) %all-to-all-start.1) | async-done | bytes 1572896 | tf_op jit(solution)/shard_map/all_to_all | solution.py:70
  51.4 4.6 %all-to-all-start = ((bf16[16,192,256]{2,1,0:T(8,128)(2,1)}), bf16[16,192,256]{2,1,0:T(8,128)(2,1)}, u32[]{:S(2)}, u32[]{:S(2)}) async-start(bf16[16,192,256]{2,1,0:T(8,128)(2,1)} %bitcast.5), calls=%async_computation | async-start | bytes 3145728 | tf_op jit(solution)/shard_map/all_to_all | solution.py:70
  56.0 0.1 eq.85
  56.1 0.1 add_select_fusion
  56.3 0.1 select_n.49
  56.4 0.1 fusion.40
  56.6 0.7 fusion.23
  57.2 0.1 copy.52
  57.3 19.3 %all-to-all-done = bf16[16,192,256]{2,1,0:T(8,128)(2,1)} async-done(((bf16[16,192,256]{2,1,0:T(8,128)(2,1)}), bf16[16,192,256]{2,1,0:T(8,128)(2,1)}, u32[]{:S(2)}, u32[]{:S(2)}) %all-to-all-start) | async-done | bytes 1572896 | tf_op jit(solution)/shard_map/all_to_all | solution.py:70
  76.6 2.1 fusion.20
  78.7 0.1 copy.49
  78.8 1.3 convolution_convert_fusion
  80.1 3.2 %convolution_convert_fusion.1 = bf16[2048,1024]{1,0:T(8,128)(2,1)} fusion(bf16[2048,256]{1,0:T(8,128)(2,1)S(1)} %bitcast.130, bf16[256,1024]{1,0:T(8,128)(2,1)S(1)} %copy-done), kind=kOutput, calls=%fused_computation.13 | convolution fusion | flops 1075838976 | bytes 5767168 | tf_op jit(solution)/shard_map/dot_general | solution.py:80
  83.3 12.7 %fusion.47 = f32[8,256,1024]{2,1,0:T(8,128)} fusion(bf16[8,256,1024]{2,1,0:T(8,128)(2,1)S(1)} %bitcast.124, bf16[8,1024,1024]{2,1,0:T(8,128)(2,1)} %param.9), kind=kOutput, calls=%fused_computation.78 | convolution fusion | flops 4294967296 | bytes 29360128 | tf_op jit(solution)/shard_map/tnp,tpq->tnq/dot_general | solution.py:82
  96.0 14.2 %fusion.5 = (f32[8,256]{1,0:T(8,128)S(1)}, f32[8,256]{1,0:T(8,128)S(1)}, bf16[8,256,1024]{2,1,0:T(8,128)(2,1)}, bf16[8,256,1024]{2,1,0:T(8,128)(2,1)}) fusion(f32[8,16,1024]{2,1,0:T(8,128)S(1)} %copy-done.1, f32[8,16,1024]{2,1,0:T(8,128)S(1)} %copy-done.2, f32[8,256,1024]{2,1,0:T(8,128)} %fusion.47, bf16[8,256,1024]{2,1,0:T(8,128)(2,1)} %bitcast.123, ...), kind=kOutput, calls=%fused_computation.11 | convolution fusion | flops 4315934720 | bytes 38813696 | tf_op jit(solution)/shard_map/tnp,tpq->tnq/dot_general | solution.py:82
  110.2 0.1 mul.88
  110.3 0.1 mul.92
  110.5 0.1 pad_maximum_fusion.1
  110.6 0.2 copy.61
  110.8 0.9 gather_fusion
  111.6 0.3 select_bitcast_fusion
  111.9 1.2 copy.55
  113.1 0.3 reshape.301
  113.4 0.6 pad.4
  114.0 8.8 %all-to-all-start.2 = ((f32[128,1,128]{2,1,0:T(1,128)}), f32[128,1,128]{2,1,0:T(1,128)S(1)}, u32[]{:S(2)}, u32[]{:S(2)}) async-start(f32[128,1,128]{2,1,0:T(1,128)} %bitcast.29), calls=%async_computation.2 | async-start | bytes 131072 | tf_op jit(solution)/shard_map/all_to_all | solution.py:121
  122.8 10.8 %convolution_convert_fusion.2 = bf16[8,256,1024]{2,1,0:T(8,128)(2,1)} fusion(bf16[8,256,1024]{2,1,0:T(8,128)(2,1)} %get-tuple-element.13, bf16[8,1024,1024]{2,1,0:T(8,128)(2,1)} %param.9), kind=kOutput, calls=%fused_computation.16 | convolution fusion | flops 4297064448 | bytes 25165824 | tf_op jit(solution)/shard_map/tnq,tpq->tnp/dot_general | solution.py:88
  133.7 3.5 %convolution_multiply_fusion = f32[2048,256]{1,0:T(8,128)S(1)} fusion(bf16[2048,1024]{1,0:T(8,128)(2,1)} %bitcast.144, bf16[256,1024]{1,0:T(8,128)(2,1)S(1)} %copy-done), kind=kOutput, calls=%fused_computation.14 | convolution fusion | flops 1074266112 | bytes 6815744 | tf_op jit(solution)/shard_map/dot_general | solution.py:94
  137.2 0.2 copy.59
  137.4 3.2 %fusion.16 = f32[8,384,256]{2,1,0:T(8,128)} fusion(f32[8,256,256]{2,1,0:T(8,128)S(1)} %bitcast.128, f32[384,256]{1,0:T(8,128)S(1)} %fusion.40), kind=kOutput, calls=%fused_computation.30 | convolution fusion | flops 1207959552 | bytes 5636096 | tf_op jit(solution)/shard_map/dot_general | solution.py:103
  140.6 10.2 %all-to-all-start.4 = ((f32[128,24,256]{2,1,0:T(8,128)}), f32[128,24,256]{2,1,0:T(8,128)}, u32[]{:S(2)}, u32[]{:S(2)}) async-start(f32[128,24,256]{2,1,0:T(8,128)} %bitcast.126), calls=%async_computation.4 | async-start | bytes 6291456 | tf_op jit(solution)/shard_map/all_to_all | solution.py:110
  150.7 10.8 %convolution_convert_fusion.3 = bf16[8,256,1024]{2,1,0:T(8,128)(2,1)} fusion(bf16[8,256,1024]{2,1,0:T(8,128)(2,1)} %get-tuple-element.12, bf16[8,1024,1024]{2,1,0:T(8,128)(2,1)} %param.9), kind=kOutput, calls=%fused_computation.17 | convolution fusion | flops 4297064448 | bytes 25165824 | tf_op jit(solution)/shard_map/tnq,tpq->tnp/dot_general | solution.py:88
  161.6 3.5 %convolution_multiply_fusion.1 = f32[2048,256]{1,0:T(8,128)S(1)} fusion(bf16[2048,1024]{1,0:T(8,128)(2,1)} %bitcast.145, bf16[256,1024]{1,0:T(8,128)(2,1)S(1)} %copy-done), kind=kOutput, calls=%fused_computation.15 | convolution fusion | flops 1074266112 | bytes 6815744 | tf_op jit(solution)/shard_map/dot_general | solution.py:94
  165.1 0.2 copy.58
  165.3 3.2 %fusion.18 = f32[8,384,256]{2,1,0:T(8,128)} fusion(f32[8,256,256]{2,1,0:T(8,128)S(1)} %bitcast.127, f32[384,256]{1,0:T(8,128)S(1)} %fusion.40), kind=kOutput, calls=%fused_computation.32 | convolution fusion | flops 1207959552 | bytes 5636096 | tf_op jit(solution)/shard_map/dot_general | solution.py:103
  168.4 23.0 %all-to-all-done.4 = f32[128,24,256]{2,1,0:T(8,128)} async-done(((f32[128,24,256]{2,1,0:T(8,128)}), f32[128,24,256]{2,1,0:T(8,128)}, u32[]{:S(2)}, u32[]{:S(2)}) %all-to-all-start.4) | async-done | bytes 3145760 | tf_op jit(solution)/shard_map/all_to_all | solution.py:110
  191.4 5.1 %all-to-all-start.3 = ((f32[128,24,256]{2,1,0:T(8,128)}), f32[128,24,256]{2,1,0:T(8,128)}, u32[]{:S(2)}, u32[]{:S(2)}) async-start(f32[128,24,256]{2,1,0:T(8,128)} %bitcast.125), calls=%async_computation.3 | async-start | bytes 6291456 | tf_op jit(solution)/shard_map/all_to_all | solution.py:110
  196.5 0.1 copy.44
  196.7 0.1 eq.81
  196.8 0.3 fusion.32
  197.0 0.6 mul.93
  197.6 0.4 copy.57
  198.1 0.1 mul.96
  198.2 0.9 mul.97
  199.1 0.3 reshape.302
  199.4 1.4 fusion.33
  200.7 2.8 %fusion.6 = f32[64,2,256]{2,0,1:T(8,128)S(1)} fusion(f32[3072,256,1]{1,0,2:T(8,128)} %bitcast.45, f32[2,3072]{1,0:T(2,128)S(1)} %mul.97, f32[64,3072]{1,0:T(8,128)S(1)} %copy.57), kind=kOutput, calls=%fused_computation.18 | convolution fusion | flops 604372992 | bytes 4087808 | tf_op jit(solution)/shard_map/dot_general | solution.py:111
  203.6 33.8 %all-to-all-done.3 = f32[128,24,256]{2,1,0:T(8,128)} async-done(((f32[128,24,256]{2,1,0:T(8,128)}), f32[128,24,256]{2,1,0:T(8,128)}, u32[]{:S(2)}, u32[]{:S(2)}) %all-to-all-start.3) | async-done | bytes 3145760 | tf_op jit(solution)/shard_map/all_to_all | solution.py:110
  237.3 2.8 %fusion.8 = f32[64,2,256]{2,0,1:T(8,128)S(1)} fusion(f32[3072,256,1]{1,0,2:T(8,128)} %bitcast.38, f32[2,3072]{1,0:T(2,128)S(1)} %mul.97, f32[64,3072]{1,0:T(8,128)S(1)} %copy.57), kind=kOutput, calls=%fused_computation.20 | convolution fusion | flops 604372992 | bytes 4087808 | tf_op jit(solution)/shard_map/dot_general | solution.py:111
  240.2 0.9 copy.60
  (20 shorter events, 0.1 us)
Async XLA Ops:
  0.6 78.2 %copy-start = (bf16[256,1024]{1,0:T(8,128)(2,1)S(1)}, bf16[256,1024]{1,0:T(8,128)(2,1)}, u32[]{:S(2)}) copy-start(bf16[256,1024]{1,0:T(8,128)(2,1)} %param.8) | copy-start | bytes 1572868
  21.4 30.0 %all-to-all-start.1 = ((bf16[16,192,256]{2,1,0:T(8,128)(2,1)}), bf16[16,192,256]{2,1,0:T(8,128)(2,1)S(1)}, u32[]{:S(2)}, u32[]{:S(2)}) async-start(bf16[16,192,256]{2,1,0:T(8,128)(2,1)} %bitcast.17), calls=%async_computation.1 | async-start | bytes 3145728 | tf_op jit(solution)/shard_map/all_to_all | solution.py:70
  28.2 2.7 %copy-start.3 = (s32[8,16]{1,0:T(8,128)S(1)}, s32[8,16]{1,0:T(8,128)}, u32[]{:S(2)}) copy-start(s32[8,16]{1,0:T(8,128)} %param.13) | copy-start | bytes 1540
  51.4 25.2 %all-to-all-start = ((bf16[16,192,256]{2,1,0:T(8,128)(2,1)}), bf16[16,192,256]{2,1,0:T(8,128)(2,1)}, u32[]{:S(2)}, u32[]{:S(2)}) async-start(bf16[16,192,256]{2,1,0:T(8,128)(2,1)} %bitcast.5), calls=%async_computation | async-start | bytes 3145728 | tf_op jit(solution)/shard_map/all_to_all | solution.py:70
  83.3 12.7 %copy-start.1 = (f32[8,16,1024]{2,1,0:T(8,128)S(1)}, f32[8,16,1024]{2,1,0:T(8,128)}, u32[]{:S(2)}) copy-start(f32[8,16,1024]{2,1,0:T(8,128)} %param.10) | copy-start | bytes 1572868
  83.3 12.7 %copy-start.2 = (f32[8,16,1024]{2,1,0:T(8,128)S(1)}, f32[8,16,1024]{2,1,0:T(8,128)}, u32[]{:S(2)}) copy-start(f32[8,16,1024]{2,1,0:T(8,128)} %param.11) | copy-start | bytes 1572868
  114.0 26.5 %all-to-all-start.2 = ((f32[128,1,128]{2,1,0:T(1,128)}), f32[128,1,128]{2,1,0:T(1,128)S(1)}, u32[]{:S(2)}, u32[]{:S(2)}) async-start(f32[128,1,128]{2,1,0:T(1,128)} %bitcast.29), calls=%async_computation.2 | async-start | bytes 131072 | tf_op jit(solution)/shard_map/all_to_all | solution.py:121
  140.6 50.8 %all-to-all-start.4 = ((f32[128,24,256]{2,1,0:T(8,128)}), f32[128,24,256]{2,1,0:T(8,128)}, u32[]{:S(2)}, u32[]{:S(2)}) async-start(f32[128,24,256]{2,1,0:T(8,128)} %bitcast.126), calls=%async_computation.4 | async-start | bytes 6291456 | tf_op jit(solution)/shard_map/all_to_all | solution.py:110
  191.4 45.9 %all-to-all-start.3 = ((f32[128,24,256]{2,1,0:T(8,128)}), f32[128,24,256]{2,1,0:T(8,128)}, u32[]{:S(2)}, u32[]{:S(2)}) async-start(f32[128,24,256]{2,1,0:T(8,128)} %bitcast.125), calls=%async_computation.3 | async-start | bytes 6291456 | tf_op jit(solution)/shard_map/all_to_all | solution.py:110

commit v3 on v2

--- a/solution.py
+++ b/solution.py
@@ -57,17 +57,22 @@
         back_select.astype(jnp.float32)[None], (expo_count,) + back_select.shape
     )
 
-    grad_pieces = []
-    like_rows = []
-    for chunk in range(N_CHUNKS):
+    def forward(chunk):
         sent = lax.dot_general(
             send_select,
             arranged[chunk],
             (((2,), (1,)), ((0,), (0,))),
             preferred_element_type=jnp.float32,
         ).astype(jnp.bfloat16)
-        sent = sent.transpose(1, 0, 2).reshape(-1, coeff_dim)
-        incoming = lax.all_to_all(sent, "sky", split_axis=0, concat_axis=0, tiled=True)
+        return sent.transpose(1, 0, 2).reshape(-1, coeff_dim)
+
+    early = []
+    grad_pieces = []
+    like_rows = []
+    for chunk in range(N_CHUNKS):
+        incoming = early.pop() if early else lax.all_to_all(
+            forward(chunk), "sky", split_axis=0, concat_axis=0, tiled=True
+        )
         by_sample = incoming.reshape(slot_count, chunk_samples, coeff_dim).transpose(1, 0, 2)
         picked = lax.dot_general(
             pick_select,
@@ -80,6 +85,9 @@
         rendered = jnp.dot(picked, basis, preferred_element_type=jnp.float32).astype(jnp.bfloat16)
         rendered = rendered.reshape(tiles_here, chunk_samples * tile_cap, pixels)
         model = jnp.einsum("tnp,tpq->tnq", rendered, operators, preferred_element_type=jnp.float32)
+        if chunk + 1 < N_CHUNKS:
+            model, sent = lax.optimization_barrier((model, forward(chunk + 1)))
+            early.append(lax.all_to_all(sent, "sky", split_axis=0, concat_axis=0, tiled=True))
         model = model.reshape(tiles_here, chunk_samples, tile_cap, pixels)
         resid = model - cutouts[:, None, :, :]
         weighted = pixel_weights[:, None, :, :] * resid

time: 242 us -> 240 us (level)
    all_to_all x0 -> x1, waiting for transfers between devices: none -> 20.4 us  [per_device(): lax.all_to_all(forward(chunk), 'sky', split_axis=0, concat_axis=0, tiled=...]
    all_to_all x2 -> x1, waiting for transfers between devices: 38.8 us -> 19 us  [per_device(): lax.all_to_all(sent, 'sky', split_axis=0, concat_axis=0, tiled=True)]
    all_to_all x2 -> x1, starting transfers between devices: 11.3 us -> 3.71 us  [per_device(): lax.all_to_all(sent, 'sky', split_axis=0, concat_axis=0, tiled=True)]
    all_to_all x0 -> x1, starting transfers between devices: none -> 6.75 us  [per_device(): lax.all_to_all(forward(chunk), 'sky', split_axis=0, concat_axis=0, tiled=...]
where the time goes in v3:
time: 240 us
  waiting for transfers between devices  96.2 us (40%)
  matrix products  75.9 us (32%)
  starting transfers between devices  34.5 us (14%)
  blocking collectives  15.7 us (7%)
  local copies, waits for them, and re-layouts  15.3 us (6%)
    all_to_all x2, waiting for transfers between devices, per_device(): lax.all_to_all(send_back, ('expo', 'sky'), split_axis=0, concat_axis=0, t...  56.7 us
    dot_general x2, matrix products, per_device(): jnp.einsum('tnp,tpq->tnq', rendered, operators, preferred_element_type=jn...  26.8 us
    dot_general x2, matrix products, per_device(): jnp.einsum('tnq,tpq->tnp', scaled, operators, preferred_element_type=jnp....  21.7 us
    all_to_all x1, waiting for transfers between devices, per_device(): lax.all_to_all(forward(chunk), 'sky', split_axis=0, concat_axis=0, tiled=...  20.4 us
    all_to_all x1, waiting for transfers between devices, per_device(): lax.all_to_all(sent, 'sky', split_axis=0, concat_axis=0, tiled=True)  19 us
    all_gather x1, blocking collectives, per_device(): lax.all_gather(detections.reshape(sky_count, send_cap), 'expo', axis=0, t...  15.7 us
    all_to_all x2, starting transfers between devices, per_device(): lax.all_to_all(send_back, ('expo', 'sky'), split_axis=0, concat_axis=0, t...  15.3 us
    all_to_all x1, starting transfers between devices, per_device(): lax.all_to_all(likes, ('expo', 'sky'), split_axis=0, concat_axis=0, tiled...  8.76 us
  transfers between devices with their start and end apart: 5, of which 4 were waited for; matrix products, arithmetic and copies ran while one was open for 20% of the time, Pallas kernels for 0%

profile of v3, /device:TPU:1, one launch (start us, length us, event | category | flops | bytes accessed | tf_op | source)
XLA Modules:
  0.0 239.6 jit_solution(11311375526521936626)
XLA Ops:
  0.6 0.0 copy-start
  0.6 15.7 %all-gather = s32[8,1,16,12]{2,1,3,0:T(1,128)S(1)} all-gather(s32[1,1,16,12]{2,1,3,0:T(1,128)} %param.12), channel_id=2, replica_groups=mesh['expo'=8,'sky'=16] {'expo'}, dimensions={0}, use_global_device_ids=true | all-gather | bytes 6912 | tf_op jit(solution)/shard_map/all_gather | solution.py:28
  16.4 0.1 copy.45
  16.5 0.1 eq.89
  16.6 1.5 reshape.292
  18.0 0.6 copy.76
  18.6 0.1 fusion.46
  18.7 0.6 fusion.26
  19.4 0.0 copy-start.3
  19.4 2.0 copy.47
  21.4 6.8 %all-to-all-start = ((bf16[16,192,256]{2,1,0:T(8,128)(2,1)}), bf16[16,192,256]{2,1,0:T(8,128)(2,1)S(1)}, u32[]{:S(2)}, u32[]{:S(2)}) async-start(bf16[16,192,256]{2,1,0:T(8,128)(2,1)} %bitcast.5), calls=%async_computation | async-start | bytes 3145728 | tf_op jit(solution)/shard_map/all_to_all | solution.py:73
  28.2 0.1 eq.85
  28.3 0.6 fusion.27
  28.9 2.1 copy.50
  31.0 20.4 %all-to-all-done = bf16[16,192,256]{2,1,0:T(8,128)(2,1)S(1)} async-done(((bf16[16,192,256]{2,1,0:T(8,128)(2,1)}), bf16[16,192,256]{2,1,0:T(8,128)(2,1)S(1)}, u32[]{:S(2)}, u32[]{:S(2)}) %all-to-all-start) | async-done | bytes 1572896 | tf_op jit(solution)/shard_map/all_to_all | solution.py:73
  51.4 0.7 fusion.20
  52.1 0.1 copy.49
  52.2 1.3 convolution_convert_fusion.1
  53.5 12.6 %fusion.47 = f32[8,256,1024]{2,1,0:T(8,128)} fusion(bf16[8,256,1024]{2,1,0:T(8,128)(2,1)S(1)} %bitcast.125, bf16[8,1024,1024]{2,1,0:T(8,128)(2,1)} %param.9), kind=kOutput, calls=%fused_computation.78 | convolution fusion | flops 4294967296 | bytes 29360128 | tf_op jit(solution)/shard_map/tnp,tpq->tnq/dot_general | solution.py:87
  66.1 3.7 %all-to-all-start.1 = ((bf16[16,192,256]{2,1,0:T(8,128)(2,1)}), bf16[16,192,256]{2,1,0:T(8,128)(2,1)S(1)}, u32[]{:S(2)}, u32[]{:S(2)}) async-start(bf16[16,192,256]{2,1,0:T(8,128)(2,1)} %bitcast.18), calls=%async_computation.1 | async-start | bytes 3145728 | tf_op jit(solution)/shard_map/all_to_all | solution.py:90
  69.8 0.1 reshape.291
  69.9 1.2 scatter_custom_fusion
  71.1 0.1 add_select_fusion
  71.2 0.1 select_n.49
  71.4 0.1 fusion.40
  71.5 19.0 %all-to-all-done.1 = bf16[16,192,256]{2,1,0:T(8,128)(2,1)S(1)} async-done(((bf16[16,192,256]{2,1,0:T(8,128)(2,1)}), bf16[16,192,256]{2,1,0:T(8,128)(2,1)S(1)}, u32[]{:S(2)}, u32[]{:S(2)}) %all-to-all-start.1) | async-done | bytes 1572896 | tf_op jit(solution)/shard_map/all_to_all | solution.py:90
  90.5 0.7 fusion.23
  91.2 0.1 copy.52
  91.3 3.2 %convolution_convert_fusion = bf16[2048,1024]{1,0:T(8,128)(2,1)} fusion(bf16[2048,256]{1,0:T(8,128)(2,1)S(1)} %bitcast.131, bf16[256,1024]{1,0:T(8,128)(2,1)S(1)} %copy-done), kind=kOutput, calls=%fused_computation.12 | convolution fusion | flops 1075838976 | bytes 5767168 | tf_op jit(solution)/shard_map/dot_general | solution.py:85
  94.5 14.2 %fusion.5 = (f32[8,256]{1,0:T(8,128)S(1)}, f32[8,256]{1,0:T(8,128)S(1)}, bf16[8,256,1024]{2,1,0:T(8,128)(2,1)}, bf16[8,256,1024]{2,1,0:T(8,128)(2,1)}) fusion(f32[8,256,1024]{2,1,0:T(8,128)} %fusion.47, f32[8,16,1024]{2,1,0:T(8,128)S(1)} %copy-done.1, f32[8,16,1024]{2,1,0:T(8,128)S(1)} %copy-done.2, bf16[8,256,1024]{2,1,0:T(8,128)(2,1)} %bitcast.124, ...), kind=kOutput, calls=%fused_computation.11 | convolution fusion | flops 4315934720 | bytes 38813696 | tf_op jit(solution)/shard_map/tnp,tpq->tnq/dot_general | solution.py:87
  108.7 0.1 mul.88
  108.8 0.1 mul.92
  109.0 0.1 pad_maximum_fusion.1
  109.1 0.2 copy.61
  109.3 0.9 gather_fusion
  110.1 0.3 select_bitcast_fusion
  110.4 1.2 copy.55
  111.6 0.3 reshape.303
  111.9 0.6 pad.4
  112.5 8.8 %all-to-all-start.2 = ((f32[128,1,128]{2,1,0:T(1,128)}), f32[128,1,128]{2,1,0:T(1,128)S(1)}, u32[]{:S(2)}, u32[]{:S(2)}) async-start(f32[128,1,128]{2,1,0:T(1,128)} %bitcast.30), calls=%async_computation.2 | async-start | bytes 131072 | tf_op jit(solution)/shard_map/all_to_all | solution.py:129
  121.3 10.8 %convolution_convert_fusion.2 = bf16[8,256,1024]{2,1,0:T(8,128)(2,1)} fusion(bf16[8,256,1024]{2,1,0:T(8,128)(2,1)} %get-tuple-element.17, bf16[8,1024,1024]{2,1,0:T(8,128)(2,1)} %param.9), kind=kOutput, calls=%fused_computation.16 | convolution fusion | flops 4297064448 | bytes 25165824 | tf_op jit(solution)/shard_map/tnq,tpq->tnp/dot_general | solution.py:96
  132.1 3.5 %convolution_multiply_fusion = f32[2048,256]{1,0:T(8,128)S(1)} fusion(bf16[2048,1024]{1,0:T(8,128)(2,1)} %bitcast.146, bf16[256,1024]{1,0:T(8,128)(2,1)S(1)} %copy-done), kind=kOutput, calls=%fused_computation.14 | convolution fusion | flops 1074266112 | bytes 6815744 | tf_op jit(solution)/shard_map/dot_general | solution.py:102
  135.6 0.2 copy.59
  135.8 3.2 %fusion.16 = f32[8,384,256]{2,1,0:T(8,128)} fusion(f32[8,256,256]{2,1,0:T(8,128)S(1)} %bitcast.129, f32[384,256]{1,0:T(8,128)S(1)} %fusion.40), kind=kOutput, calls=%fused_computation.30 | convolution fusion | flops 1207959552 | bytes 5636096 | tf_op jit(solution)/shard_map/dot_general | solution.py:111
  139.0 10.2 %all-to-all-start.4 = ((f32[128,24,256]{2,1,0:T(8,128)}), f32[128,24,256]{2,1,0:T(8,128)}, u32[]{:S(2)}, u32[]{:S(2)}) async-start(f32[128,24,256]{2,1,0:T(8,128)} %bitcast.127), calls=%async_computation.4 | async-start | bytes 6291456 | tf_op jit(solution)/shard_map/all_to_all | solution.py:118
  149.2 10.8 %convolution_convert_fusion.3 = bf16[8,256,1024]{2,1,0:T(8,128)(2,1)} fusion(bf16[8,256,1024]{2,1,0:T(8,128)(2,1)} %get-tuple-element.16, bf16[8,1024,1024]{2,1,0:T(8,128)(2,1)} %param.9), kind=kOutput, calls=%fused_computation.17 | convolution fusion | flops 4297064448 | bytes 25165824 | tf_op jit(solution)/shard_map/tnq,tpq->tnp/dot_general | solution.py:96
  160.0 3.5 %convolution_multiply_fusion.1 = f32[2048,256]{1,0:T(8,128)S(1)} fusion(bf16[2048,1024]{1,0:T(8,128)(2,1)} %bitcast.147, bf16[256,1024]{1,0:T(8,128)(2,1)S(1)} %copy-done), kind=kOutput, calls=%fused_computation.15 | convolution fusion | flops 1074266112 | bytes 6815744 | tf_op jit(solution)/shard_map/dot_general | solution.py:102
  163.5 0.2 copy.58
  163.7 3.2 %fusion.18 = f32[8,384,256]{2,1,0:T(8,128)} fusion(f32[8,256,256]{2,1,0:T(8,128)S(1)} %bitcast.128, f32[384,256]{1,0:T(8,128)S(1)} %fusion.40), kind=kOutput, calls=%fused_computation.32 | convolution fusion | flops 1207959552 | bytes 5636096 | tf_op jit(solution)/shard_map/dot_general | solution.py:111
  166.9 23.0 %all-to-all-done.4 = f32[128,24,256]{2,1,0:T(8,128)} async-done(((f32[128,24,256]{2,1,0:T(8,128)}), f32[128,24,256]{2,1,0:T(8,128)}, u32[]{:S(2)}, u32[]{:S(2)}) %all-to-all-start.4) | async-done | bytes 3145760 | tf_op jit(solution)/shard_map/all_to_all | solution.py:118
  189.9 5.1 %all-to-all-start.3 = ((f32[128,24,256]{2,1,0:T(8,128)}), f32[128,24,256]{2,1,0:T(8,128)}, u32[]{:S(2)}, u32[]{:S(2)}) async-start(f32[128,24,256]{2,1,0:T(8,128)} %bitcast.126), calls=%async_computation.3 | async-start | bytes 6291456 | tf_op jit(solution)/shard_map/all_to_all | solution.py:118
  195.0 0.1 copy.44
  195.1 0.1 eq.81
  195.2 0.3 fusion.32
  195.5 0.6 mul.93
  196.1 0.4 copy.57
  196.6 0.1 mul.96
  196.7 0.9 mul.97
  197.6 0.3 reshape.304
  197.8 1.4 fusion.33
  199.2 2.8 %fusion.6 = f32[64,2,256]{2,0,1:T(8,128)S(1)} fusion(f32[3072,256,1]{1,0,2:T(8,128)} %bitcast.46, f32[2,3072]{1,0:T(2,128)S(1)} %mul.97, f32[64,3072]{1,0:T(8,128)S(1)} %copy.57), kind=kOutput, calls=%fused_computation.18 | convolution fusion | flops 604372992 | bytes 4087808 | tf_op jit(solution)/shard_map/dot_general | solution.py:119
  202.0 33.8 %all-to-all-done.3 = f32[128,24,256]{2,1,0:T(8,128)} async-done(((f32[128,24,256]{2,1,0:T(8,128)}), f32[128,24,256]{2,1,0:T(8,128)}, u32[]{:S(2)}, u32[]{:S(2)}) %all-to-all-start.3) | async-done | bytes 3145760 | tf_op jit(solution)/shard_map/all_to_all | solution.py:118
  235.8 2.8 %fusion.8 = f32[64,2,256]{2,0,1:T(8,128)S(1)} fusion(f32[3072,256,1]{1,0,2:T(8,128)} %bitcast.39, f32[2,3072]{1,0:T(2,128)S(1)} %mul.97, f32[64,3072]{1,0:T(8,128)S(1)} %copy.57), kind=kOutput, calls=%fused_computation.20 | convolution fusion | flops 604372992 | bytes 4087808 | tf_op jit(solution)/shard_map/dot_general | solution.py:119
  238.7 0.9 copy.60
  (20 shorter events, 0.1 us)
Async XLA Ops:
  0.6 51.6 %copy-start = (bf16[256,1024]{1,0:T(8,128)(2,1)S(1)}, bf16[256,1024]{1,0:T(8,128)(2,1)}, u32[]{:S(2)}) copy-start(bf16[256,1024]{1,0:T(8,128)(2,1)} %param.8) | copy-start | bytes 1572868
  19.4 8.8 %copy-start.3 = (s32[8,16]{1,0:T(8,128)S(1)}, s32[8,16]{1,0:T(8,128)}, u32[]{:S(2)}) copy-start(s32[8,16]{1,0:T(8,128)} %param.13) | copy-start | bytes 1540
  21.4 30.0 %all-to-all-start = ((bf16[16,192,256]{2,1,0:T(8,128)(2,1)}), bf16[16,192,256]{2,1,0:T(8,128)(2,1)S(1)}, u32[]{:S(2)}, u32[]{:S(2)}) async-start(bf16[16,192,256]{2,1,0:T(8,128)(2,1)} %bitcast.5), calls=%async_computation | async-start | bytes 3145728 | tf_op jit(solution)/shard_map/all_to_all | solution.py:73
  66.1 24.4 %all-to-all-start.1 = ((bf16[16,192,256]{2,1,0:T(8,128)(2,1)}), bf16[16,192,256]{2,1,0:T(8,128)(2,1)S(1)}, u32[]{:S(2)}, u32[]{:S(2)}) async-start(bf16[16,192,256]{2,1,0:T(8,128)(2,1)} %bitcast.18), calls=%async_computation.1 | async-start | bytes 3145728 | tf_op jit(solution)/shard_map/all_to_all | solution.py:90
  91.3 3.2 %copy-start.1 = (f32[8,16,1024]{2,1,0:T(8,128)S(1)}, f32[8,16,1024]{2,1,0:T(8,128)}, u32[]{:S(2)}) copy-start(f32[8,16,1024]{2,1,0:T(8,128)} %param.10) | copy-start | bytes 1572868
  91.3 3.2 %copy-start.2 = (f32[8,16,1024]{2,1,0:T(8,128)S(1)}, f32[8,16,1024]{2,1,0:T(8,128)}, u32[]{:S(2)}) copy-start(f32[8,16,1024]{2,1,0:T(8,128)} %param.11) | copy-start | bytes 1572868
  112.5 26.5 %all-to-all-start.2 = ((f32[128,1,128]{2,1,0:T(1,128)}), f32[128,1,128]{2,1,0:T(1,128)S(1)}, u32[]{:S(2)}, u32[]{:S(2)}) async-start(f32[128,1,128]{2,1,0:T(1,128)} %bitcast.30), calls=%async_computation.2 | async-start | bytes 131072 | tf_op jit(solution)/shard_map/all_to_all | solution.py:129
  139.0 50.9 %all-to-all-start.4 = ((f32[128,24,256]{2,1,0:T(8,128)}), f32[128,24,256]{2,1,0:T(8,128)}, u32[]{:S(2)}, u32[]{:S(2)}) async-start(f32[128,24,256]{2,1,0:T(8,128)} %bitcast.127), calls=%async_computation.4 | async-start | bytes 6291456 | tf_op jit(solution)/shard_map/all_to_all | solution.py:118
  189.9 45.9 %all-to-all-start.3 = ((f32[128,24,256]{2,1,0:T(8,128)}), f32[128,24,256]{2,1,0:T(8,128)}, u32[]{:S(2)}, u32[]{:S(2)}) async-start(f32[128,24,256]{2,1,0:T(8,128)} %bitcast.126), calls=%async_computation.3 | async-start | bytes 6291456 | tf_op jit(solution)/shard_map/all_to_all | solution.py:118
